TPU v7x, 32 devices: a whole 2x2x4 slice. The times are simulated.
32 devices in a mesh: axial: 8 (over y, x, core), radial: 4 (over z).
Axes of the slice: x: 2, y: 2, z: 4, core: 2. Of those that a mesh axis runs over, the one named last changes fastest.
Arguments:
- composition_deviations: float32 [38, 1024, 512], P(None, 'axial', 'radial'), may hold values from -6 to 6
- flow_speed_vector: float32 [2, 1024, 512], P(None, 'axial', 'radial'), may hold values from -1 to 1
- thermal_field: float32 [1024, 512], P('axial', 'radial'), may hold values from 0.4 to 4
- linearized_kinetics_operator: float32 [38, 38], replicated, may hold values from -0.5 to 0.5
- frozen_jacobian_inverse_addend: float32 [38, 38], replicated, may hold values from -0.25 to 0.25
- rigid_block_indicator: int32 [512, 4], P('axial', 'radial'), may hold values from 0 to 1, as said below
- molar_absorptivity_table: float32 [4, 38], replicated, may hold values from -1 to 1
- spokewise_sightline_length: float32 [512], P('radial'), may hold values from 0.3 to 3
- sightline_lengthwise_index: int32 [4, 32768], replicated, may hold values from 0 to 1023
- observed_absorbance_traces: float32 [4, 32768], P(None, ('axial', 'radial')), may hold values from -6 to 6
Outputs:
- species_out: float32 [38, 1024, 512], P(None, 'axial', 'radial')
- misfit: float32 [4, 32768], P(None, ('axial', 'radial'))
Inputs may be any that keep to these rules, and one draw needn't show every extreme that they name: `rigid_block_indicator`: in each radial column of tiles, the tiles of 2 cyclically consecutive axial devices are all stiff and every other axial device holds exactly 8 stiff tiles, so the column holds 176 stiff tiles.
All inputs are finite; a program needn't handle non-finite values.
Results may differ from a plain program's by a relative error of at most 0.0001.
Values sent between devices are 32-bit elements; how exact they have to be, the bound alone decides.
No kernel may reach another device: no remote copies, remote signals or barrier semaphores. Data moves between devices by JAX's collectives and lax.ppermute only.
A program may use at most 192 MiB of HBM per device.

v0:
```python
import math
import jax
import jax.numpy as jnp
from jax import lax
from jax.sharding import PartitionSpec as P

TILE_ROWS = 2
ITERS = 3
TIME_STEP = 0.4
CHEM_STEP = 0.5
ARRHENIUS_BARRIER = 1.0
WENO_EPS = 1e-06
HIGHEST = lax.Precision.HIGHEST


def extended(shard, sides, width):
    for axis, dim in sides:
        peers, length = (lax.axis_size(axis), shard.shape[dim])
        up = [(i, (i + 1) % peers) for i in range(peers - 1)]
        down = [(j, i) for i, j in up]
        last = lax.slice_in_dim(shard, length - width, length, axis=dim)
        initial = lax.slice_in_dim(shard, 0, width, axis=dim)
        before = lax.ppermute(last, axis, up)
        after = lax.ppermute(initial, axis, down)
        shard = jnp.concatenate([before, shard, after], axis=dim)
    return shard


def weno_side(minus_two, minus_one, centre, plus_one, plus_two):
    beta_zero = (
        13.0 / 12.0 * (minus_two - 2.0 * minus_one + centre) ** 2
        + 0.25 * (minus_two - 4.0 * minus_one + 3.0 * centre) ** 2
    )
    beta_one = (
        13.0 / 12.0 * (minus_one - 2.0 * centre + plus_one) ** 2
        + 0.25 * (minus_one - plus_one) ** 2
    )
    beta_two = (
        13.0 / 12.0 * (centre - 2.0 * plus_one + plus_two) ** 2
        + 0.25 * (3.0 * centre - 4.0 * plus_one + plus_two) ** 2
    )
    weight_zero = 0.1 / (WENO_EPS + beta_zero) ** 2
    weight_one = 0.6 / (WENO_EPS + beta_one) ** 2
    weight_two = 0.3 / (WENO_EPS + beta_two) ** 2
    weight_total = weight_zero + weight_one + weight_two
    blended = weight_zero * (2.0 * minus_two - 7.0 * minus_one + 11.0 * centre)
    blended = blended + weight_one * (-minus_one + 5.0 * centre + 2.0 * plus_one)
    blended = blended + weight_two * (2.0 * centre + 5.0 * plus_one - plus_two)
    return blended / (6.0 * weight_total)


def face_difference(field, speed, along, length):
    face_count = length + 1

    def cut_part(offset):
        return lax.slice_in_dim(field, offset, offset + face_count, axis=along)

    left_value = weno_side(cut_part(0), cut_part(1), cut_part(2), cut_part(3), cut_part(4))
    right_value = weno_side(cut_part(5), cut_part(4), cut_part(3), cut_part(2), cut_part(1))
    face_speed = 0.5 * (
        lax.slice_in_dim(speed, 2, 2 + face_count, axis=along)
        + lax.slice_in_dim(speed, 3, 3 + face_count, axis=along)
    )
    face_flux = (
        jnp.maximum(face_speed, 0.0) * left_value + jnp.minimum(face_speed, 0.0) * right_value
    )
    return lax.slice_in_dim(face_flux, 1, face_count, axis=along) - lax.slice_in_dim(
        face_flux, 0, face_count - 1, axis=along
    )


def transport(field_pad, speed_pad):
    row_count = field_pad.shape[1] - 6
    col_count = field_pad.shape[2] - 6
    along_axial = face_difference(field_pad[:, :, 3:-3], speed_pad[0:1, :, 3:-3], 1, row_count)
    along_radial = face_difference(field_pad[:, 3:-3, :], speed_pad[1:2, 3:-3, :], 2, col_count)
    return field_pad[:, 3:-3, 3:-3] - TIME_STEP * (along_axial + along_radial)


def kinetics_advance(
    starting_composition_field,
    thermal_field,
    linearized_kinetics_operator,
    frozen_jacobian_inverse_addend,
):
    acceleration_factor = jnp.exp(-ARRHENIUS_BARRIER / thermal_field)
    current = starting_composition_field
    for newton_step in range(ITERS):
        source = jnp.tensordot(
            linearized_kinetics_operator, current, axes=(1, 0), precision=HIGHEST
        ) - jnp.tanh(current)
        defect = current - starting_composition_field - CHEM_STEP * acceleration_factor * source
        current = (
            current
            - defect
            - jnp.tensordot(frozen_jacobian_inverse_addend, defect, axes=(1, 0), precision=HIGHEST)
        )
    return current


def absorbance_profile(field, molar_absorptivity_table, spokewise_sightline_length):
    mixed = jnp.tensordot(molar_absorptivity_table, field, axes=(1, 0), precision=HIGHEST)
    return jnp.dot(mixed, spokewise_sightline_length, precision=HIGHEST)


def local(
    composition_deviations,
    flow_speed_vector,
    thermal_field,
    linearized_kinetics_operator,
    frozen_jacobian_inverse_addend,
    rigid_block_indicator,
    molar_absorptivity_table,
    spokewise_sightline_length,
    sightline_lengthwise_index,
    observed_absorbance_traces,
):
    species_count = composition_deviations.shape[0]
    stacked = jnp.concatenate([composition_deviations, flow_speed_vector], axis=0)
    padded = extended(stacked, (("axial", 1), ("radial", 2)), 3)
    advected_composition_field = transport(padded[:species_count], padded[species_count:])
    combusted_composition_field = kinetics_advance(
        advected_composition_field,
        thermal_field,
        linearized_kinetics_operator,
        frozen_jacobian_inverse_addend,
    )
    flag_cells = jnp.repeat(
        jnp.repeat(rigid_block_indicator, TILE_ROWS, axis=0),
        advected_composition_field.shape[2],
        axis=1,
    )
    species_out = jnp.where(
        flag_cells[None] > 0, combusted_composition_field, advected_composition_field
    )
    path_scale = 1.0 / math.sqrt(advected_composition_field.shape[2] * lax.axis_size("radial"))
    profile = (
        absorbance_profile(species_out, molar_absorptivity_table, spokewise_sightline_length)
        * path_scale
    )
    column = lax.psum(profile, "radial")
    whole_profile = lax.all_gather(column, "axial", axis=1, tiled=True)
    device = lax.axis_index(("axial", "radial"))
    sample_count = observed_absorbance_traces.shape[1]
    own_rows = lax.dynamic_slice_in_dim(
        sightline_lengthwise_index, device * sample_count, sample_count, 1
    )
    values = jnp.take_along_axis(whole_profile, own_rows, axis=1)
    return (species_out, values - observed_absorbance_traces)


def solution(mesh):
    in_specs = (
        P(None, "axial", "radial"),
        P(None, "axial", "radial"),
        P("axial", "radial"),
        P(),
        P(),
        P("axial", "radial"),
        P(),
        P("radial"),
        P(),
        P(None, ("axial", "radial")),
    )
    out_specs = (P(None, "axial", "radial"), P(None, ("axial", "radial")))
    return jax.shard_map(local, mesh=mesh, in_specs=in_specs, out_specs=out_specs, check_vma=False)
```

profile of v0, /device:TPU:0, one launch (start us, length us, event | category | flops | bytes accessed | tf_op | source)
XLA Modules:
  0.0 168.7 jit_solution(240044641915545838)
XLA Ops:
  0.7 2.6 %copy.75 = f32[38,128,128]{1,0,2:T(8,128)S(1)} copy(f32[38,128,128]{2,1,0:T(8,128)} %param.10) | data formatting | bytes 4980736 | tf_op args[0]
  3.4 3.3 %slice_maximum_fusion = (f32[40,3,128]{1,0,2:T(8,128)}, f32[40,3,128]{1,0,2:T(8,128)}) fusion(f32[2,128,128]{1,0,2:T(2,128)S(1)} %copy.64, f32[38,128,128]{1,0,2:T(8,128)S(1)} %copy.75), kind=kLoop, calls=%fused_computation.63 | loop fusion | flops 30720 | bytes 2744320 | tf_op jit(solution)/shard_map/concatenate | solution.py:119
  6.7 2.5 %copy.67 = f32[40,3,128]{2,0,1:T(8,128)S(1)} copy(f32[40,3,128]{1,0,2:T(8,128)} %get-tuple-element.25) | data formatting | bytes 122880 | tf_op jit(solution)/shard_map/slice | solution.py:22
  10.5 2.5 %copy.65 = f32[40,3,128]{2,0,1:T(8,128)S(1)} copy(f32[40,3,128]{1,0,2:T(8,128)} %get-tuple-element.24) | data formatting | bytes 122880 | tf_op jit(solution)/shard_map/slice | solution.py:21
  13.1 3.0 %collective-permute-start = (f32[40,3,128]{2,0,1:T(8,128)S(1)}, f32[40,3,128]{2,0,1:T(8,128)S(1)}, u32[]{:S(2)}, u32[]{:S(2)}) collective-permute-start(f32[40,3,128]{2,0,1:T(8,128)S(1)} %copy.65), channel_id=1, source_target_pairs={{0,4},{4,8},{8,12},{12,16},{16,20},{20,24},{24,28},{1,5},{5,9},{9,... | collective-permute-start | bytes 184328 | tf_op jit(solution)/shard_map/ppermute | solution.py:23
  17.3 2.3 %copy.68 = f32[40,3,128]{1,0,2:T(8,128)} copy(f32[40,3,128]{2,0,1:T(8,128)S(1)} %collective-permute-done.1) | data formatting | bytes 122880 | tf_op jit(solution)/shard_map/ppermute | solution.py:24
  19.6 2.3 %copy.66 = f32[40,3,128]{1,0,2:T(8,128)} copy(f32[40,3,128]{2,0,1:T(8,128)S(1)} %collective-permute-done) | data formatting | bytes 122880 | tf_op jit(solution)/shard_map/ppermute | solution.py:23
  24.5 2.7 %maximum_maximum_fusion.1 = (f32[40,131,128]{1,0,2:T(8,128)S(1)}, f32[40,131,128]{1,0,2:T(8,128)S(1)}) fusion(f32[2,128,128]{1,0,2:T(2,128)S(1)} %copy.64, f32[38,128,128]{1,0,2:T(8,128)S(1)} %copy.75, f32[40,3,128]{1,0,2:T(8,128)S(1)} %copy-done.2, f32[40,3,128]{1,0,2:T(8,128)S(1)} %copy-done.1), kind=kLoop, calls=%fused_computation.3 | loop fusion | flops 2682880 | bytes 8110080 | tf_op jit(solution)/shard_map/concatenate | solution.py:25
  28.0 4.9 %collective-permute-start.2 = (f32[40,134,3]{1,0,2:T(8,128)S(1)}, f32[40,134,3]{1,0,2:T(8,128)S(1)}, u32[]{:S(2)}, u32[]{:S(2)}) collective-permute-start(f32[40,134,3]{1,0,2:T(8,128)S(1)} %get-tuple-element.20), channel_id=1, source_target_pairs={{0,1},{1,2},{2,3},{4,5},{5,6},{6,7},{8,9},{9,10},{10,11},{12,13},{... | collective-permute-start | bytes 192968 | tf_op jit(solution)/shard_map/ppermute | solution.py:23
  34.5 25.3 %multiply_add_fusion = f32[38,129,128]{1,0,2:T(8,128)} fusion(f32[40,131,128]{1,0,2:T(8,128)S(1)} %get-tuple-element.23, f32[40,131,128]{1,0,2:T(8,128)S(1)} %get-tuple-element.22, f32[129,128]{0,1:T(8,128)S(1)} %get-tuple-element.28, f32[129,128]{0,1:T(8,128)S(1)} %get-tuple-element.29), kind=kLoop, calls=%fused_computation.5 | loop fusion | flops 77177088 | bytes 17700864 | tf_op jit(solution)/shard_map/add | solution.py:65
  60.2 7.2 %maximum_maximum_fusion = (f32[40,134,131]{1,0,2:T(8,128)S(1)}, f32[40,134,131]{1,0,2:T(8,128)S(1)}) fusion(f32[40,3,128]{1,0,2:T(8,128)S(1)} %copy-done.1, f32[2,128,128]{1,0,2:T(2,128)S(1)} %copy.64, f32[38,128,128]{1,0,2:T(8,128)S(1)} %copy.75, f32[40,3,128]{1,0,2:T(8,128)S(1)} %copy-done.2, f32[40,134,3]{1,0,2:T(8,128)S(1)} %collective-permute-done.2, ...), kind=kLoop, calls=%fused_computation.1 | loop fusion | flops 5617280 | bytes 8490240 | tf_op jit(solution)/shard_map/concatenate | solution.py:25
  67.4 13.0 %multiply_add_fusion.3 = f32[38,128,129]{1,0,2:T(8,128)S(1)} fusion(f32[40,134,131]{1,0,2:T(8,128)S(1)} %get-tuple-element.19, f32[40,134,131]{1,0,2:T(8,128)S(1)} %get-tuple-element.18, f32[128,129]{0,1:T(8,128)S(1)} %get-tuple-element.26, f32[128,129]{0,1:T(8,128)S(1)} %get-tuple-element.27), kind=kLoop, calls=%fused_computation.31 | loop fusion | flops 77177088 | bytes 17700864 | tf_op jit(solution)/shard_map/add | solution.py:65
  80.5 4.3 %fusion.44 = f32[38,128,128]{1,0,2:T(8,128)S(1)} fusion(f32[38,128,128]{1,0,2:T(8,128)S(1)} %copy.75, f32[38,128,129]{1,0,2:T(8,128)S(1)} %multiply_add_fusion.3, f32[38,129,128]{1,0,2:T(8,128)} %multiply_add_fusion), kind=kLoop, calls=%fused_computation.60 | loop fusion | flops 3112960 | bytes 14942208 | tf_op jit(solution)/shard_map/sub | solution.py:77
  84.8 2.5 %fusion.78 = f32[128,128,38]{0,2,1:T(8,128)S(1)} fusion(f32[38,128,128]{1,0,2:T(8,128)S(1)} %fusion.44, f32[38,38]{1,0:T(8,128)S(1)} %copy-done), kind=kOutput, calls=%fused_computation.113 | convolution fusion | flops 283901952 | bytes 4986512 | tf_op jit(solution)/shard_map/dot_general | solution.py:89
  87.3 4.1 %bitcast_subtract_fusion.4 = f32[38,128,128]{1,0,2:T(8,128)S(1)} fusion(f32[38,128,128]{1,0,2:T(8,128)S(1)} %fusion.44, f32[128,128,38]{0,2,1:T(8,128)S(1)} %fusion.78, f32[128,128]{0,1:T(8,128)S(1)} %copy.76, f32[38,38]{1,0:T(8,128)S(1)} %copy-done.4), kind=kOutput, calls=%fused_computation.73 | convolution fusion | flops 290127872 | bytes 7542416 | tf_op jit(solution)/shard_map/dot_general | solution.py:96
  91.4 2.4 %fusion.76 = f32[128,128,38]{0,2,1:T(8,128)S(1)} fusion(f32[38,128,128]{1,0,2:T(8,128)S(1)} %bitcast_subtract_fusion.4, f32[38,38]{1,0:T(8,128)S(1)} %copy-done), kind=kOutput, calls=%fused_computation.111 | convolution fusion | flops 283901952 | bytes 4986512 | tf_op jit(solution)/shard_map/dot_general | solution.py:89
  93.8 4.5 %bitcast_subtract_fusion.2 = f32[38,128,128]{1,0,2:T(8,128)S(1)} fusion(f32[38,128,128]{1,0,2:T(8,128)S(1)} %bitcast_subtract_fusion.4, f32[128,128,38]{0,2,1:T(8,128)S(1)} %fusion.76, f32[38,128,128]{1,0,2:T(8,128)S(1)} %fusion.44, f32[128,128]{0,1:T(8,128)S(1)} %copy.76, f32[38,38]{1,0:T(8,128)S(1)} %copy-done.4), kind=kOutput, calls=%fused_computation.69 | convolution fusion | flops 290127872 | bytes 10032784 | tf_op jit(solution)/shard_map/dot_general | solution.py:96
  98.3 2.3 %fusion.74 = f32[128,128,38]{0,2,1:T(8,128)S(1)} fusion(f32[38,128,128]{1,0,2:T(8,128)S(1)} %bitcast_subtract_fusion.2, f32[38,38]{1,0:T(8,128)S(1)} %copy-done), kind=kOutput, calls=%fused_computation.109 | convolution fusion | flops 283901952 | bytes 4986512 | tf_op jit(solution)/shard_map/dot_general | solution.py:89
  100.6 4.4 %fusion.45 = f32[38,128,128]{1,0,2:T(8,128)S(1)} fusion(f32[38,128,128]{1,0,2:T(8,128)S(1)} %fusion.44, f32[38,128,128]{1,0,2:T(8,128)S(1)} %bitcast_subtract_fusion.2, f32[128,128,38]{0,2,1:T(8,128)S(1)} %fusion.74, f32[128,128]{0,1:T(8,128)S(1)} %copy.76, pred[128]{0:T(512)(128)(4,1)S(1)} %gt.22, f32[38,38]{1,0:T(8,128)S(1)} %copy-done.4), kind=kOutput, calls=%fused_computation.65 | convolution fusion | flops 290750464 | bytes 10032912 | tf_op jit(solution)/shard_map/dot_general | solution.py:96
  104.9 2.1 %copy.77 = f32[38,128,128]{2,1,0:T(8,128)} copy(f32[38,128,128]{1,0,2:T(8,128)S(1)} %fusion.45) | data formatting | bytes 4980736
  107.1 1.7 %convolution_bitcast_fusion = f32[4,128,128]{1,0,2:T(4,128)S(1)} fusion(f32[38,128,128]{1,0,2:T(8,128)S(1)} %fusion.45, f32[4,38]{1,0:T(4,128)S(1)} %copy-done.7), kind=kOutput, calls=%fused_computation.85 | convolution fusion | flops 29884416 | bytes 2753120 | tf_op jit(solution)/shard_map/dot_general | solution.py:102
  109.1 13.0 %psum.7 = f32[4,128]{1,0:T(4,128)S(1)} all-reduce(f32[4,128]{1,0:T(4,128)S(1)} %broadcast_multiply_fusion), channel_id=1, replica_groups=mesh['axial'=8,'radial'=4] {'radial'}, use_global_device_ids=true, to_apply=%region_0.1 | all-reduce | flops 512 | bytes 4096 | tf_op jit(solution)/shard_map/psum | solution.py:141
  122.1 10.3 %all_gather.3 = f32[4,1024]{1,0:T(4,128)S(1)} all-gather(f32[4,128]{1,0:T(4,128)S(1)} %psum.7), channel_id=1, replica_groups=mesh['axial'=8,'radial'=4] {'axial'}, dimensions={1}, use_global_device_ids=true | all-gather | bytes 18432 | tf_op jit(solution)/shard_map/all_gather | solution.py:142
  132.4 35.0 %gather_fusion = f32[4096]{0:T(1024)S(1)} fusion(f32[4,1024]{1,0:T(4,128)S(1)} %all_gather.3, s32[4096]{0:T(1024)S(1)} %bitcast.92), kind=kCustom, calls=%fused_computation | custom fusion | bytes 65536 | tf_op jit(solution)/shard_map/jit(take_along_axis)/gather | solution.py:148
  (45 shorter events, 9.6 us)
Async XLA Ops:
  0.6 84.1 %copy-start = (f32[38,38]{1,0:T(8,128)S(1)}, f32[38,38]{1,0:T(8,128)}, u32[]{:S(2)}) copy-start(f32[38,38]{1,0:T(8,128)} %param.13) | copy-start | bytes 17332
  0.6 2.6 %copy-start.3 = (f32[2,128,128]{2,1,0:T(8,128)S(1)}, f32[2,128,128]{2,1,0:T(8,128)}, u32[]{:S(2)}) copy-start(f32[2,128,128]{2,1,0:T(8,128)} %param.11) | copy-start | bytes 393220
  6.7 9.4 %copy-start.5 = (f32[128,128]{1,0:T(8,128)S(1)}, f32[128,128]{1,0:T(8,128)}, u32[]{:S(2)}) copy-start(f32[128,128]{1,0:T(8,128)} %param.12) | copy-start | bytes 196612
  6.7 9.6 %copy-start.9 = (s32[64,1]{0,1:T(1,128)S(1)}, s32[64,1]{0,1:T(1,128)}, u32[]{:S(2)}) copy-start(s32[64,1]{0,1:T(1,128)} %param.15) | copy-start | bytes 772
  9.2 8.0 %collective-permute-start.1 = (f32[40,3,128]{2,0,1:T(8,128)S(1)}, f32[40,3,128]{2,0,1:T(8,128)S(1)}, u32[]{:S(2)}, u32[]{:S(2)}) collective-permute-start(f32[40,3,128]{2,0,1:T(8,128)S(1)} %copy.67), channel_id=1, source_target_pairs={{4,0},{8,4},{12,8},{16,12},{20,16},{24,20},{28,24},{5,1},{9,5},{13... | collective-permute-start | bytes 184328 | tf_op jit(solution)/shard_map/ppermute | solution.py:24
  13.1 6.5 %collective-permute-start = (f32[40,3,128]{2,0,1:T(8,128)S(1)}, f32[40,3,128]{2,0,1:T(8,128)S(1)}, u32[]{:S(2)}, u32[]{:S(2)}) collective-permute-start(f32[40,3,128]{2,0,1:T(8,128)S(1)} %copy.65), channel_id=1, source_target_pairs={{0,4},{4,8},{8,12},{12,16},{16,20},{20,24},{24,28},{1,5},{5,9},{9,... | collective-permute-start | bytes 184328 | tf_op jit(solution)/shard_map/ppermute | solution.py:23
  21.9 1.9 %copy-start.1 = (f32[40,3,128]{1,0,2:T(8,128)S(1)}, f32[40,3,128]{1,0,2:T(8,128)}, u32[]{:S(2)}) copy-start(f32[40,3,128]{1,0,2:T(8,128)} %copy.68) | copy-start | bytes 184324
  21.9 2.6 %copy-start.2 = (f32[40,3,128]{1,0,2:T(8,128)S(1)}, f32[40,3,128]{1,0,2:T(8,128)}, u32[]{:S(2)}) copy-start(f32[40,3,128]{1,0,2:T(8,128)} %copy.66) | copy-start | bytes 184324
  28.0 31.9 %collective-permute-start.2 = (f32[40,134,3]{1,0,2:T(8,128)S(1)}, f32[40,134,3]{1,0,2:T(8,128)S(1)}, u32[]{:S(2)}, u32[]{:S(2)}) collective-permute-start(f32[40,134,3]{1,0,2:T(8,128)S(1)} %get-tuple-element.20), channel_id=1, source_target_pairs={{0,1},{1,2},{2,3},{4,5},{5,6},{6,7},{8,9},{9,10},{10,11},{12,13},{... | collective-permute-start | bytes 192968 | tf_op jit(solution)/shard_map/ppermute | solution.py:23
  32.9 26.9 %collective-permute-start.3 = (f32[40,134,3]{1,0,2:T(8,128)S(1)}, f32[40,134,3]{1,0,2:T(8,128)S(1)}, u32[]{:S(2)}, u32[]{:S(2)}) collective-permute-start(f32[40,134,3]{1,0,2:T(8,128)S(1)} %get-tuple-element.21), channel_id=1, source_target_pairs={{1,0},{2,1},{3,2},{5,4},{6,5},{7,6},{9,8},{10,9},{11,10},{13,12},{... | collective-permute-start | bytes 192968 | tf_op jit(solution)/shard_map/ppermute | solution.py:24
  84.8 2.5 %copy-start.4 = (f32[38,38]{1,0:T(8,128)S(1)}, f32[38,38]{1,0:T(8,128)}, u32[]{:S(2)}) copy-start(f32[38,38]{1,0:T(8,128)} %param.14) | copy-start | bytes 17332
  104.9 2.1 %copy-start.7 = (f32[4,38]{1,0:T(4,128)S(1)}, f32[4,38]{1,0:T(4,128)}, u32[]{:S(2)}) copy-start(f32[4,38]{1,0:T(4,128)} %param.16) | copy-start | bytes 1828
  107.1 1.7 %copy-start.8 = (f32[128]{0:T(128)S(1)}, f32[128]{0:T(128)}, u32[]{:S(2)}) copy-start(f32[128]{0:T(128)} %param.17) | copy-start | bytes 1540
  132.4 35.0 %copy-start.6 = (f32[4,1024]{1,0:T(4,128)S(1)}, f32[4,1024]{1,0:T(4,128)}, u32[]{:S(2)}) copy-start(f32[4,1024]{1,0:T(4,128)} %param.19) | copy-start | bytes 49156
where the time goes:
time: 169 us
  other arithmetic  60.4 us (36%)
  local copies, waits for them, and re-layouts  51.3 us (30%)
  blocking collectives  23.3 us (14%)
  matrix products  22.1 us (13%)
  starting transfers between devices  10.7 us (6%)
    add x2, other arithmetic, face_difference(): jnp.maximum(face_speed, 0.0) * left_value  38.3 us
    gather x2, local copies, waits for them, and re-layouts, local(): values = jnp.take_along_axis(whole_profile, own_rows, axis=1)  35 us
    psum x1, blocking collectives, local(): column = lax.psum(profile, 'radial')  13 us
    dot_general x3, matrix products, kinetics_advance(): jnp.tensordot(frozen_jacobian_inverse_addend, defect, axes=(1, 0), precis...  13 us
    all_gather x1, blocking collectives, local(): whole_profile = lax.all_gather(column, 'axial', axis=1, tiled=True)  10.3 us
    concatenate x2, other arithmetic, extended(): shard = jnp.concatenate([before, shard, after], axis=dim)  9.84 us
    ppermute x2, starting transfers between devices, extended(): before = lax.ppermute(last, axis, up)  7.97 us
    dot_general x3, matrix products, kinetics_advance(): jnp.tensordot(linearized_kinetics_operator, current, axes=(1, 0), precisi...  7.12 us
  transfers between devices with their start and end apart: 4, of which 0 were waited for; matrix products, arithmetic and copies ran while one was open for 19% of the time, Pallas kernels for 0%

commit v1 on v0

--- a/solution.py
+++ b/solution.py
@@ -139,7 +139,9 @@
         * path_scale
     )
     column = lax.psum(profile, "radial")
-    whole_profile = lax.all_gather(column, "axial", axis=1, tiled=True)
+    local_out = jnp.stack(lax.axis_size("axial") * [column])
+    arr_next = lax.all_to_all(local_out, "axial", 0, 0)
+    whole_profile = jnp.concatenate(arr_next, axis=1)
     device = lax.axis_index(("axial", "radial"))
     sample_count = observed_absorbance_traces.shape[1]
     own_rows = lax.dynamic_slice_in_dim(

time: 169 us -> 166 us (0.982)
  blocking collectives: 23.3 us -> 13 us
  starting transfers between devices: 10.7 us -> 15.7 us
  local copies, waits for them, and re-layouts: 51.3 us -> 53.2 us
    all_gather x1 -> x0, blocking collectives: 10.3 us -> none  [local(): whole_profile = lax.all_gather(column, 'axial', axis=1, tiled=True)]
    all_to_all x0 -> x1, starting transfers between devices: none -> 4.97 us  [local(): arr_next = lax.all_to_all(local_out, 'axial', 0, 0)]
    unnamed x25 -> x27, local copies, waits for them, and re-layouts: 6.29 us -> 7.52 us
  transfers between devices with their start and end apart: 4 -> 5, of which waited for: 0 -> 1; matrix products, arithmetic and copies ran while one was open for 19% -> 21% of each run, Pallas kernels for 0% -> 0%
where the time goes in v1:
time: 166 us
  other arithmetic  60.4 us (36%)
  local copies, waits for them, and re-layouts  53.2 us (32%)
  matrix products  22.1 us (13%)
  starting transfers between devices  15.7 us (9%)
  blocking collectives  13 us (8%)
    add x2, other arithmetic, face_difference(): jnp.maximum(face_speed, 0.0) * left_value  38.3 us
    gather x2, local copies, waits for them, and re-layouts, local(): values = jnp.take_along_axis(whole_profile, own_rows, axis=1)  35 us
    psum x1, blocking collectives, local(): column = lax.psum(profile, 'radial')  13 us
    dot_general x3, matrix products, kinetics_advance(): jnp.tensordot(frozen_jacobian_inverse_addend, defect, axes=(1, 0), precis...  13 us
    concatenate x2, other arithmetic, extended(): shard = jnp.concatenate([before, shard, after], axis=dim)  9.84 us
    ppermute x2, starting transfers between devices, extended(): before = lax.ppermute(last, axis, up)  7.97 us
    unnamed x27, local copies, waits for them, and re-layouts  7.52 us
    dot_general x3, matrix products, kinetics_advance(): jnp.tensordot(linearized_kinetics_operator, current, axes=(1, 0), precisi...  7.12 us
  transfers between devices with their start and end apart: 5, of which 1 were waited for; matrix products, arithmetic and copies ran while one was open for 21% of the time, Pallas kernels for 0%

profile of v1, /device:TPU:0, one launch (start us, length us, event | category | flops | bytes accessed | tf_op | source)
XLA Modules:
  0.0 166.0 jit_solution(7243457039256928961)
XLA Ops:
  0.7 2.6 %copy.75 = f32[38,128,128]{1,0,2:T(8,128)S(1)} copy(f32[38,128,128]{2,1,0:T(8,128)} %param.10) | data formatting | bytes 4980736 | tf_op args[0]
  3.4 3.3 %slice_maximum_fusion = (f32[40,3,128]{1,0,2:T(8,128)}, f32[40,3,128]{1,0,2:T(8,128)}) fusion(f32[2,128,128]{1,0,2:T(2,128)S(1)} %copy.64, f32[38,128,128]{1,0,2:T(8,128)S(1)} %copy.75), kind=kLoop, calls=%fused_computation.63 | loop fusion | flops 30720 | bytes 2744320 | tf_op jit(solution)/shard_map/concatenate | solution.py:119
  6.7 2.5 %copy.67 = f32[40,3,128]{2,0,1:T(8,128)S(1)} copy(f32[40,3,128]{1,0,2:T(8,128)} %get-tuple-element.25) | data formatting | bytes 122880 | tf_op jit(solution)/shard_map/slice | solution.py:22
  10.6 2.5 %copy.65 = f32[40,3,128]{2,0,1:T(8,128)S(1)} copy(f32[40,3,128]{1,0,2:T(8,128)} %get-tuple-element.24) | data formatting | bytes 122880 | tf_op jit(solution)/shard_map/slice | solution.py:21
  13.1 3.0 %collective-permute-start = (f32[40,3,128]{2,0,1:T(8,128)S(1)}, f32[40,3,128]{2,0,1:T(8,128)S(1)}, u32[]{:S(2)}, u32[]{:S(2)}) collective-permute-start(f32[40,3,128]{2,0,1:T(8,128)S(1)} %copy.65), channel_id=1, source_target_pairs={{0,4},{4,8},{8,12},{12,16},{16,20},{20,24},{24,28},{1,5},{5,9},{9,... | collective-permute-start | bytes 184328 | tf_op jit(solution)/shard_map/ppermute | solution.py:23
  16.5 2.3 %copy.68 = f32[40,3,128]{1,0,2:T(8,128)} copy(f32[40,3,128]{2,0,1:T(8,128)S(1)} %collective-permute-done.1) | data formatting | bytes 122880 | tf_op jit(solution)/shard_map/ppermute | solution.py:24
  18.8 2.3 %copy.66 = f32[40,3,128]{1,0,2:T(8,128)} copy(f32[40,3,128]{2,0,1:T(8,128)S(1)} %collective-permute-done) | data formatting | bytes 122880 | tf_op jit(solution)/shard_map/ppermute | solution.py:23
  23.8 2.7 %maximum_maximum_fusion.1 = (f32[40,131,128]{1,0,2:T(8,128)S(1)}, f32[40,131,128]{1,0,2:T(8,128)S(1)}) fusion(f32[2,128,128]{1,0,2:T(2,128)S(1)} %copy.64, f32[38,128,128]{1,0,2:T(8,128)S(1)} %copy.75, f32[40,3,128]{1,0,2:T(8,128)S(1)} %copy-done.2, f32[40,3,128]{1,0,2:T(8,128)S(1)} %copy-done.1), kind=kLoop, calls=%fused_computation.3 | loop fusion | flops 2682880 | bytes 8110080 | tf_op jit(solution)/shard_map/concatenate | solution.py:25
  27.3 4.9 %collective-permute-start.2 = (f32[40,134,3]{1,0,2:T(8,128)S(1)}, f32[40,134,3]{1,0,2:T(8,128)S(1)}, u32[]{:S(2)}, u32[]{:S(2)}) collective-permute-start(f32[40,134,3]{1,0,2:T(8,128)S(1)} %get-tuple-element.20), channel_id=1, source_target_pairs={{0,1},{1,2},{2,3},{4,5},{5,6},{6,7},{8,9},{9,10},{10,11},{12,13},{... | collective-permute-start | bytes 192968 | tf_op jit(solution)/shard_map/ppermute | solution.py:23
  33.8 25.3 %multiply_add_fusion = f32[38,129,128]{1,0,2:T(8,128)} fusion(f32[40,131,128]{1,0,2:T(8,128)S(1)} %get-tuple-element.23, f32[40,131,128]{1,0,2:T(8,128)S(1)} %get-tuple-element.22, f32[129,128]{0,1:T(8,128)S(1)} %get-tuple-element.28, f32[129,128]{0,1:T(8,128)S(1)} %get-tuple-element.29), kind=kLoop, calls=%fused_computation.5 | loop fusion | flops 77177088 | bytes 17700864 | tf_op jit(solution)/shard_map/add | solution.py:65
  59.6 7.2 %maximum_maximum_fusion = (f32[40,134,131]{1,0,2:T(8,128)S(1)}, f32[40,134,131]{1,0,2:T(8,128)S(1)}) fusion(f32[40,3,128]{1,0,2:T(8,128)S(1)} %copy-done.1, f32[2,128,128]{1,0,2:T(2,128)S(1)} %copy.64, f32[38,128,128]{1,0,2:T(8,128)S(1)} %copy.75, f32[40,3,128]{1,0,2:T(8,128)S(1)} %copy-done.2, f32[40,134,3]{1,0,2:T(8,128)S(1)} %collective-permute-done.2, ...), kind=kLoop, calls=%fused_computation.1 | loop fusion | flops 5617280 | bytes 8490240 | tf_op jit(solution)/shard_map/concatenate | solution.py:25
  66.7 13.0 %multiply_add_fusion.3 = f32[38,128,129]{1,0,2:T(8,128)S(1)} fusion(f32[40,134,131]{1,0,2:T(8,128)S(1)} %get-tuple-element.19, f32[40,134,131]{1,0,2:T(8,128)S(1)} %get-tuple-element.18, f32[128,129]{0,1:T(8,128)S(1)} %get-tuple-element.26, f32[128,129]{0,1:T(8,128)S(1)} %get-tuple-element.27), kind=kLoop, calls=%fused_computation.31 | loop fusion | flops 77177088 | bytes 17700864 | tf_op jit(solution)/shard_map/add | solution.py:65
  79.8 4.3 %fusion.44 = f32[38,128,128]{1,0,2:T(8,128)S(1)} fusion(f32[38,128,128]{1,0,2:T(8,128)S(1)} %copy.75, f32[38,128,129]{1,0,2:T(8,128)S(1)} %multiply_add_fusion.3, f32[38,129,128]{1,0,2:T(8,128)} %multiply_add_fusion), kind=kLoop, calls=%fused_computation.60 | loop fusion | flops 3112960 | bytes 14942208 | tf_op jit(solution)/shard_map/sub | solution.py:77
  84.1 2.5 %fusion.78 = f32[128,128,38]{0,2,1:T(8,128)S(1)} fusion(f32[38,128,128]{1,0,2:T(8,128)S(1)} %fusion.44, f32[38,38]{1,0:T(8,128)S(1)} %copy-done), kind=kOutput, calls=%fused_computation.113 | convolution fusion | flops 283901952 | bytes 4986512 | tf_op jit(solution)/shard_map/dot_general | solution.py:89
  86.6 4.1 %bitcast_subtract_fusion.4 = f32[38,128,128]{1,0,2:T(8,128)S(1)} fusion(f32[38,128,128]{1,0,2:T(8,128)S(1)} %fusion.44, f32[128,128,38]{0,2,1:T(8,128)S(1)} %fusion.78, f32[128,128]{0,1:T(8,128)S(1)} %copy.76, f32[38,38]{1,0:T(8,128)S(1)} %copy-done.5), kind=kOutput, calls=%fused_computation.73 | convolution fusion | flops 290127872 | bytes 7542416 | tf_op jit(solution)/shard_map/dot_general | solution.py:96
  90.7 2.4 %fusion.76 = f32[128,128,38]{0,2,1:T(8,128)S(1)} fusion(f32[38,128,128]{1,0,2:T(8,128)S(1)} %bitcast_subtract_fusion.4, f32[38,38]{1,0:T(8,128)S(1)} %copy-done), kind=kOutput, calls=%fused_computation.111 | convolution fusion | flops 283901952 | bytes 4986512 | tf_op jit(solution)/shard_map/dot_general | solution.py:89
  93.1 4.5 %bitcast_subtract_fusion.2 = f32[38,128,128]{1,0,2:T(8,128)S(1)} fusion(f32[38,128,128]{1,0,2:T(8,128)S(1)} %bitcast_subtract_fusion.4, f32[128,128,38]{0,2,1:T(8,128)S(1)} %fusion.76, f32[38,128,128]{1,0,2:T(8,128)S(1)} %fusion.44, f32[128,128]{0,1:T(8,128)S(1)} %copy.76, f32[38,38]{1,0:T(8,128)S(1)} %copy-done.5), kind=kOutput, calls=%fused_computation.69 | convolution fusion | flops 290127872 | bytes 10032784 | tf_op jit(solution)/shard_map/dot_general | solution.py:96
  97.6 2.3 %fusion.74 = f32[128,128,38]{0,2,1:T(8,128)S(1)} fusion(f32[38,128,128]{1,0,2:T(8,128)S(1)} %bitcast_subtract_fusion.2, f32[38,38]{1,0:T(8,128)S(1)} %copy-done), kind=kOutput, calls=%fused_computation.109 | convolution fusion | flops 283901952 | bytes 4986512 | tf_op jit(solution)/shard_map/dot_general | solution.py:89
  99.9 4.4 %fusion.45 = f32[38,128,128]{1,0,2:T(8,128)S(1)} fusion(f32[38,128,128]{1,0,2:T(8,128)S(1)} %fusion.44, f32[38,128,128]{1,0,2:T(8,128)S(1)} %bitcast_subtract_fusion.2, f32[128,128,38]{0,2,1:T(8,128)S(1)} %fusion.74, f32[128,128]{0,1:T(8,128)S(1)} %copy.76, pred[128]{0:T(512)(128)(4,1)S(1)} %gt.22, f32[38,38]{1,0:T(8,128)S(1)} %copy-done.5), kind=kOutput, calls=%fused_computation.65 | convolution fusion | flops 290750464 | bytes 10032912 | tf_op jit(solution)/shard_map/dot_general | solution.py:96
  104.3 1.7 %convolution_bitcast_fusion = f32[4,128,128]{1,0,2:T(4,128)S(1)} fusion(f32[38,128,128]{1,0,2:T(8,128)S(1)} %fusion.45, f32[4,38]{1,0:T(4,128)S(1)} %copy-done.8), kind=kOutput, calls=%fused_computation.85 | convolution fusion | flops 29884416 | bytes 2753120 | tf_op jit(solution)/shard_map/dot_general | solution.py:102
  106.3 13.0 %psum.7 = f32[4,128]{1,0:T(4,128)S(1)} all-reduce(f32[4,128]{1,0:T(4,128)S(1)} %broadcast_multiply_fusion), channel_id=1, replica_groups=mesh['axial'=8,'radial'=4] {'radial'}, use_global_device_ids=true, to_apply=%region_0.1 | all-reduce | flops 512 | bytes 4096 | tf_op jit(solution)/shard_map/psum | solution.py:141
  119.9 5.0 %all-to-all-start = ((f32[8,4,128]{2,1,0:T(4,128)}), f32[8,4,128]{2,1,0:T(4,128)S(1)}, u32[]{:S(2)}, u32[]{:S(2)}) async-start(f32[8,4,128]{2,1,0:T(4,128)} %stack.2), calls=%async_computation | async-start | bytes 32768 | tf_op jit(solution)/shard_map/all_to_all | solution.py:143
  125.6 3.4 %copy.77 = f32[38,128,128]{2,1,0:T(8,128)} copy(f32[38,128,128]{1,0,2:T(8,128)} %copy-done.3) | data formatting | bytes 4980736
  129.6 35.0 %gather_fusion = f32[4096]{0:T(1024)S(1)} fusion(f32[4,1024]{1,0:T(4,128)S(1)} %bitcast.95, s32[4096]{0:T(1024)S(1)} %bitcast.96), kind=kCustom, calls=%fused_computation | custom fusion | bytes 65536 | tf_op jit(solution)/shard_map/jit(take_along_axis)/gather | solution.py:150
  (49 shorter events, 10.9 us)
Async XLA Ops:
  0.6 83.4 %copy-start = (f32[38,38]{1,0:T(8,128)S(1)}, f32[38,38]{1,0:T(8,128)}, u32[]{:S(2)}) copy-start(f32[38,38]{1,0:T(8,128)} %param.13) | copy-start | bytes 17332
  0.6 2.6 %copy-start.4 = (f32[2,128,128]{2,1,0:T(8,128)S(1)}, f32[2,128,128]{2,1,0:T(8,128)}, u32[]{:S(2)}) copy-start(f32[2,128,128]{2,1,0:T(8,128)} %param.11) | copy-start | bytes 393220
  6.7 9.4 %copy-start.6 = (f32[128,128]{1,0:T(8,128)S(1)}, f32[128,128]{1,0:T(8,128)}, u32[]{:S(2)}) copy-start(f32[128,128]{1,0:T(8,128)} %param.12) | copy-start | bytes 196612
  6.7 9.5 %copy-start.10 = (s32[64,1]{0,1:T(1,128)S(1)}, s32[64,1]{0,1:T(1,128)}, u32[]{:S(2)}) copy-start(s32[64,1]{0,1:T(1,128)} %param.15) | copy-start | bytes 772
  9.3 7.3 %collective-permute-start.1 = (f32[40,3,128]{2,0,1:T(8,128)S(1)}, f32[40,3,128]{2,0,1:T(8,128)S(1)}, u32[]{:S(2)}, u32[]{:S(2)}) collective-permute-start(f32[40,3,128]{2,0,1:T(8,128)S(1)} %copy.67), channel_id=1, source_target_pairs={{4,0},{8,4},{12,8},{16,12},{20,16},{24,20},{28,24},{5,1},{9,5},{13... | collective-permute-start | bytes 184328 | tf_op jit(solution)/shard_map/ppermute | solution.py:24
  13.1 5.8 %collective-permute-start = (f32[40,3,128]{2,0,1:T(8,128)S(1)}, f32[40,3,128]{2,0,1:T(8,128)S(1)}, u32[]{:S(2)}, u32[]{:S(2)}) collective-permute-start(f32[40,3,128]{2,0,1:T(8,128)S(1)} %copy.65), channel_id=1, source_target_pairs={{0,4},{4,8},{8,12},{12,16},{16,20},{20,24},{24,28},{1,5},{5,9},{9,... | collective-permute-start | bytes 184328 | tf_op jit(solution)/shard_map/ppermute | solution.py:23
  21.2 1.9 %copy-start.1 = (f32[40,3,128]{1,0,2:T(8,128)S(1)}, f32[40,3,128]{1,0,2:T(8,128)}, u32[]{:S(2)}) copy-start(f32[40,3,128]{1,0,2:T(8,128)} %copy.68) | copy-start | bytes 184324
  21.2 2.6 %copy-start.2 = (f32[40,3,128]{1,0,2:T(8,128)S(1)}, f32[40,3,128]{1,0,2:T(8,128)}, u32[]{:S(2)}) copy-start(f32[40,3,128]{1,0,2:T(8,128)} %copy.66) | copy-start | bytes 184324
  27.3 31.9 %collective-permute-start.2 = (f32[40,134,3]{1,0,2:T(8,128)S(1)}, f32[40,134,3]{1,0,2:T(8,128)S(1)}, u32[]{:S(2)}, u32[]{:S(2)}) collective-permute-start(f32[40,134,3]{1,0,2:T(8,128)S(1)} %get-tuple-element.20), channel_id=1, source_target_pairs={{0,1},{1,2},{2,3},{4,5},{5,6},{6,7},{8,9},{9,10},{10,11},{12,13},{... | collective-permute-start | bytes 192968 | tf_op jit(solution)/shard_map/ppermute | solution.py:23
  32.2 26.9 %collective-permute-start.3 = (f32[40,134,3]{1,0,2:T(8,128)S(1)}, f32[40,134,3]{1,0,2:T(8,128)S(1)}, u32[]{:S(2)}, u32[]{:S(2)}) collective-permute-start(f32[40,134,3]{1,0,2:T(8,128)S(1)} %get-tuple-element.21), channel_id=1, source_target_pairs={{1,0},{2,1},{3,2},{5,4},{6,5},{7,6},{9,8},{10,9},{11,10},{13,12},{... | collective-permute-start | bytes 192968 | tf_op jit(solution)/shard_map/ppermute | solution.py:24
  84.1 2.5 %copy-start.5 = (f32[38,38]{1,0:T(8,128)S(1)}, f32[38,38]{1,0:T(8,128)}, u32[]{:S(2)}) copy-start(f32[38,38]{1,0:T(8,128)} %param.14) | copy-start | bytes 17332
  99.9 4.4 %copy-start.8 = (f32[4,38]{1,0:T(4,128)S(1)}, f32[4,38]{1,0:T(4,128)}, u32[]{:S(2)}) copy-start(f32[4,38]{1,0:T(4,128)} %param.16) | copy-start | bytes 1828
  104.3 15.6 %copy-start.3 = (f32[38,128,128]{1,0,2:T(8,128)}, f32[38,128,128]{1,0,2:T(8,128)S(1)}, u32[]{:S(2)}) copy-start(f32[38,128,128]{1,0,2:T(8,128)S(1)} %fusion.45) | copy-start | bytes 7471108
  104.3 1.7 %copy-start.9 = (f32[128]{0:T(128)S(1)}, f32[128]{0:T(128)}, u32[]{:S(2)}) copy-start(f32[128]{0:T(128)} %param.17) | copy-start | bytes 1540
  119.9 9.7 %all-to-all-start = ((f32[8,4,128]{2,1,0:T(4,128)}), f32[8,4,128]{2,1,0:T(4,128)S(1)}, u32[]{:S(2)}, u32[]{:S(2)}) async-start(f32[8,4,128]{2,1,0:T(4,128)} %stack.2), calls=%async_computation | async-start | bytes 32768 | tf_op jit(solution)/shard_map/all_to_all | solution.py:143
  129.6 35.0 %copy-start.7 = (f32[4,1024]{1,0:T(4,128)S(1)}, f32[4,1024]{1,0:T(4,128)}, u32[]{:S(2)}) copy-start(f32[4,1024]{1,0:T(4,128)} %param.19) | copy-start | bytes 49156
